TPU v7x, 32 devices: a whole 2x2x4 slice. The times are simulated.
32 devices in a mesh: groups: 2 (over y), seq: 4 (over z), head: 2 (over x), sub: 2 (over core).
Axes of the slice: x: 2, y: 2, z: 4, core: 2. Of those that a mesh axis runs over, the one named last changes fastest.
Arguments:
- queries: bfloat16 [64, 1024, 128], P(('head', 'sub'), ('groups', 'seq')), parts along dimension 1, may hold values from -6 to 6
- keys_values: bfloat16 [8, 1024, 256], P(('head', 'sub'), ('groups', 'seq')), parts along dimension 1, may hold values from -6 to 6
- student_x: bfloat16 [64, 1024, 128], P(('head', 'sub'), ('groups', 'seq')), parts along dimension 1, may hold values from -32 to 32
- state_maps: bfloat16 [8, 1024, 128], P(('head', 'sub'), ('groups', 'seq')), parts along dimension 1, may hold values from -0.75 to 0.75
- decay_logit: float32 [64, 1024], P(('head', 'sub'), ('groups', 'seq')), parts along dimension 1, may hold values from 0 to 16
- skip_gain: float32 [64], P(('head', 'sub')), may hold values from 0.5 to 2
- init_state: float32 [128, 64, 128], P(('groups', 'head', 'sub')), parts along dimension 0, may hold values from -6 to 6
Outputs:
- grad_x: bfloat16 [64, 1024, 128], P(('head', 'sub'), ('groups', 'seq')), parts along dimension 1
- grad_maps: bfloat16 [8, 1024, 128], P(('head', 'sub'), ('groups', 'seq')), parts along dimension 1
- grad_log_decay: float32 [64, 1024], P(('head', 'sub'), ('groups', 'seq')), parts along dimension 1
There are 2 independent parts, one for each index of `groups`. A program takes and returns all parts, laid end to end along the dimension named above; an argument that names none is the same for every part. Nothing has to cross between parts.
All inputs are finite; a program needn't handle non-finite values.
Results may differ from a plain program's by a relative error of at most 0.013.
Values may be sent and summed in bfloat16 or wider, within the bound.
No kernel may reach another device: no remote copies, remote signals or barrier semaphores. Data moves between devices by JAX's collectives and lax.ppermute only.
A program may use at most 64 MiB of HBM per device.

v0:
```python
import math
import jax
import jax.numpy as jnp
from jax import lax
from jax.sharding import PartitionSpec as P

epsilon = 1e-05
highest = lax.Precision.HIGHEST


def entering_2(x, axis, join, neutral):
    place = lax.axis_index(axis)
    gathered = jax.tree.map(
        lambda a, kind: lax.all_gather(a.astype(kind), axis), x, (jnp.bfloat16, jnp.bfloat16)
    )
    state = jax.tree.map(lambda a, e: jnp.zeros_like(a) + jnp.asarray(e, a.dtype), x, neutral)

    def entering_one(turn, state):
        return join(
            state,
            jax.tree.map(
                lambda a, own: lax.dynamic_index_in_dim(a, turn, 0, False).astype(own.dtype),
                gathered,
                x,
            ),
        )

    return lax.fori_loop(0, place, entering_one, state)


def prefix(x, axis, join, neutral):
    count = lax.axis_size(axis)
    place = lax.axis_index(axis)
    ahead = count - 1 - place
    gathered = jax.tree.map(
        lambda a, kind: lax.all_gather(a.astype(kind), axis),
        x,
        jax.tree.map(lambda a: jnp.bfloat16 if a.dtype == jnp.float32 else a.dtype, x),
    )
    state = jax.tree.map(lambda a, e: jnp.zeros_like(a) + jnp.asarray(e, a.dtype), x, neutral)

    def prefix_one(turn, state):
        source = count - 1 - turn
        return join(
            state,
            jax.tree.map(
                lambda a, own: lax.dynamic_index_in_dim(a, source, 0, False).astype(own.dtype),
                gathered,
                x,
            ),
        )

    return lax.fori_loop(0, ahead, prefix_one, state)


def attend(query_rows, positions, keys_values, tok_dev):
    group_count, row_count, head_width = query_rows.shape
    score_scale = head_width ** (-0.5)
    start_max = jnp.full((group_count, row_count), -1e30, jnp.float32)
    start_sum = jnp.zeros((group_count, row_count), jnp.float32)
    start_acc = jnp.zeros((group_count, row_count, head_width), jnp.float32)
    shards = lax.all_gather(keys_values, "seq", axis=1, tiled=True)
    block_rows = math.gcd(shards.shape[1], tok_dev)

    def one_block(number, running):
        running_max, running_sum, weighted = running
        key_block = lax.dynamic_slice_in_dim(shards, number * block_rows, block_rows, 1)
        scores = (
            jnp.einsum(
                "grd,gkd->grk",
                query_rows,
                key_block[:, :, :head_width],
                preferred_element_type=jnp.float32,
            )
            * score_scale
        )
        key_positions = number * block_rows + jnp.arange(block_rows)
        allowed = (positions[:, None] >= key_positions[None, :])[None]
        scores = jnp.where(allowed, scores, -1e30)
        new_max = jnp.maximum(running_max, jnp.max(scores, axis=2))
        weights = jnp.where(allowed, jnp.exp(scores - new_max[..., None]), 0.0)
        factor = jnp.exp(running_max - new_max)
        running_sum = running_sum * factor + jnp.sum(weights, axis=2)
        weighted = weighted * factor[..., None] + jnp.einsum(
            "grk,gkd->grd",
            weights.astype(jnp.bfloat16),
            key_block[:, :, head_width:],
            preferred_element_type=jnp.float32,
        )
        return (new_max, running_sum, weighted)

    running_max, running_sum, weighted = lax.fori_loop(
        0, shards.shape[1] // block_rows, one_block, (start_max, start_sum, start_acc)
    )
    return (weighted / running_sum[..., None]).astype(jnp.bfloat16)


def forward_chain(earlier, later):
    return (earlier[0] * later[0], later[0][:, None, None] * earlier[1] + later[1])


def backward_chain(earlier, later):
    decay_early, state_early, closing_early, sums_early = earlier
    decay_late, state_late, closing_late, sums_late = later
    return (
        decay_early * decay_late,
        decay_late[:, None, None] * state_early + state_late,
        closing_early + decay_early[:, None, None] * closing_late,
        sums_early + sums_late - jnp.sum(closing_late * state_early, axis=(1, 2)),
    )


def body(queries, keys_values, student_x, state_maps, decay_logit, skip_gain, init_state):
    local_heads, tok_dev, head_width = student_x.shape
    local_groups = state_maps.shape[0]
    per_group = local_heads // local_groups
    state_size = state_maps.shape[2] // 2
    seq_count = lax.axis_size("seq")
    seq_rank = lax.axis_index("seq")
    repeat_count = max(1, seq_count // per_group)
    sub_rows = tok_dev // repeat_count
    per_peer = per_group * repeat_count // seq_count
    sectioned = queries.reshape(local_groups, per_group * repeat_count, sub_rows, head_width)
    arrived = lax.all_to_all(sectioned, "seq", split_axis=1, concat_axis=1, tiled=True)
    slot_ids = jnp.arange(seq_count * per_peer)
    source = slot_ids // per_peer
    member = seq_rank * per_peer + slot_ids % per_peer
    starts = source * tok_dev + member % repeat_count * sub_rows
    positions = (starts[:, None] + jnp.arange(sub_rows)[None, :]).reshape(-1)
    answers = attend(arrived.reshape(local_groups, -1, head_width), positions, keys_values, tok_dev)
    answers = answers.reshape(local_groups, seq_count * per_peer, sub_rows, head_width)
    teacher = lax.all_to_all(answers, "seq", split_axis=1, concat_axis=1, tiled=True).reshape(
        local_heads, tok_dev, head_width
    )
    teacher_wide = teacher.astype(jnp.float32)
    target = teacher_wide * lax.rsqrt(
        jnp.mean(teacher_wide * teacher_wide, axis=2, keepdims=True) + epsilon
    )
    log_decay = jax.nn.log_sigmoid(decay_logit)
    cumulative = jnp.cumsum(log_decay, axis=1)
    totals = cumulative[:, -1]
    decays = jnp.exp(totals)
    to_end = jnp.exp(totals[:, None] - cumulative)
    from_start = jnp.exp(cumulative)
    in_maps = state_maps[:, :, :state_size]
    out_maps = state_maps[:, :, state_size:]
    intersection = jnp.einsum("gtn,gsn->gts", out_maps, in_maps, preferred_element_type=jnp.float32)
    order_ids = jnp.arange(tok_dev)
    causal = (order_ids[:, None] >= order_ids[None, :])[None]
    gaps = cumulative[:, :, None] - cumulative[:, None, :]
    decayed = jnp.where(causal, jnp.exp(jnp.where(causal, gaps, 0.0)), 0.0)
    mixing = (
        decayed.reshape(local_groups, per_group, tok_dev, tok_dev) * intersection[:, None]
    ).reshape(local_heads, tok_dev, tok_dev)
    inputs_wide = student_x.astype(jnp.float32)
    in_heads = jnp.repeat(in_maps.astype(jnp.float32), per_group, axis=0)
    out_heads = jnp.repeat(out_maps.astype(jnp.float32), per_group, axis=0)
    local_out = jnp.einsum("hts,hsp->htp", mixing, inputs_wide, precision=highest)
    weighted_in = in_heads * to_end[..., None]
    end_state = jnp.einsum("hsn,hsp->hnp", weighted_in, inputs_wide, precision=highest)
    prefix_decay, prefix_state = entering_2(
        (decays, end_state),
        "seq",
        forward_chain,
        (jnp.ones_like(decays), jnp.zeros_like(end_state)),
    )
    entering = prefix_state + prefix_decay[:, None, None] * init_state
    state_out = local_out + from_start[..., None] * jnp.einsum(
        "htn,hnp->htp", out_heads, entering, precision=highest
    )
    outputs = state_out + skip_gain[:, None, None] * inputs_wide
    inverse = lax.rsqrt(jnp.mean(outputs * outputs, axis=2, keepdims=True) + epsilon)
    normed = outputs * inverse
    residual = normed - target
    grad_out = (residual - normed * jnp.mean(residual * normed, axis=2, keepdims=True)) * inverse
    local_dx = jnp.einsum("hts,htp->hsp", mixing, grad_out, precision=highest)
    cross = jnp.einsum("htp,hsp->hts", grad_out, inputs_wide, precision=highest)
    paired = decayed * cross
    local_din = jnp.einsum("hts,htn->hsn", paired, out_heads, precision=highest)
    grad_output_maps = jnp.einsum("hts,hsn->htn", paired, in_heads, precision=highest)
    grad_output_maps = grad_output_maps + from_start[..., None] * jnp.einsum(
        "hnp,htp->htn", entering, grad_out, precision=highest
    )
    forward_term = jnp.sum(grad_out * state_out, axis=2)
    flow = jnp.einsum(
        "htn,htp->hnp", out_heads * from_start[..., None], grad_out, precision=highest
    )
    closing = jnp.sum(forward_term - jnp.sum(inputs_wide * local_dx, axis=2), axis=1)
    identity = (
        jnp.ones_like(decays),
        jnp.zeros_like(flow),
        jnp.zeros_like(end_state),
        jnp.zeros_like(closing),
    )
    unused_decay, incoming, unused_state, later_sum = prefix(
        (decays, flow, end_state, closing), "seq", backward_chain, identity
    )
    state_dx = local_dx + jnp.einsum("hsn,hnp->hsp", weighted_in, incoming, precision=highest)
    terms = forward_term - jnp.sum(inputs_wide * state_dx, axis=2)
    grad_log_decay = later_sum[:, None] + lax.cumsum(terms, axis=1, reverse=True)
    grad_input_maps = (
        local_din
        + jnp.einsum("hnp,hsp->hsn", incoming, inputs_wide, precision=highest) * to_end[..., None]
    )
    grad_maps = jnp.concatenate([grad_input_maps, grad_output_maps], axis=2)
    grad_maps = grad_maps.reshape(local_groups, per_group, tok_dev, 2 * state_size).sum(axis=1)
    grad_x = state_dx + skip_gain[:, None, None] * grad_out
    return (grad_x.astype(jnp.bfloat16), grad_maps.astype(jnp.bfloat16), grad_log_decay)


def solution(mesh):
    in_specs = (
        P(("head", "sub"), ("groups", "seq"), None),
        P(("head", "sub"), ("groups", "seq"), None),
        P(("head", "sub"), ("groups", "seq"), None),
        P(("head", "sub"), ("groups", "seq"), None),
        P(("head", "sub"), ("groups", "seq")),
        P(("head", "sub")),
        P(("groups", "head", "sub"), None, None),
    )
    out_specs = (
        P(("head", "sub"), ("groups", "seq"), None),
        P(("head", "sub"), ("groups", "seq"), None),
        P(("head", "sub"), ("groups", "seq")),
    )
    return jax.shard_map(body, mesh=mesh, in_specs=in_specs, out_specs=out_specs, check_vma=False)
```

profile of v0, /device:TPU:0, one launch (start us, length us, event | category | flops | bytes accessed | tf_op | source)
XLA Modules:
  0.0 146.4 jit_solution(11512429082375482874)
XLA Ops:
  7.2 0.8 fusion.37
  8.9 1.2 convolution_convert_fusion.1
  10.1 0.8 copy.89
  10.9 6.3 %all-to-all-start = ((bf16[2,8,128,128]{3,2,0,1:T(8,128)(2,1)}), bf16[2,8,128,128]{3,2,0,1:T(8,128)(2,1)S(1)}, u32[]{:S(2)}, u32[]{:S(2)}) async-start(bf16[2,8,128,128]{3,2,0,1:T(8,128)(2,1)} %copy.89), calls=%async_computation | async-start | bytes 1048576 | tf_op jit(solution)/shard_map/all_to_all | solution.py:124
  17.8 0.6 copy-done.19
  18.5 0.6 dynamic-slice
  19.9 18.1 %all-reduce = bf16[64]{0:T(256)(128)(2,1)S(1)} all-reduce(bf16[64]{0:T(256)(128)(2,1)S(1)} %dynamic-update-slice), channel_id=2, replica_groups=mesh['groups'=2,'seq'=4,'head'=2,'sub'=2] {'seq'}, use_global_device_ids=true, to_apply=%add | all-reduce | flops 64 | bytes 256
  38.4 0.3 bitcast_multiply_fusion.1
  38.8 0.5 copy-done.17
  39.3 23.4 %all_gather.30 = bf16[2,512,256]{2,1,0:T(8,128)(2,1)} all-gather(bf16[2,128,256]{2,1,0:T(8,128)(2,1)S(1)} %copy-done.17), channel_id=1, replica_groups=mesh['groups'=2,'seq'=4,'head'=2,'sub'=2] {'seq'}, dimensions={1}, use_global_device_ids=true | all-gather | bytes 655360 | tf_op jit(solution)/shard_map/all_gather | solution.py:62
  62.8 2.2 %fusion.49 = f32[16,128,128]{1,2,0:T(8,128)} fusion(f32[16,128,128]{2,1,0:T(8,128)S(1)} %bitcast_multiply_fusion.1, bf16[16,128,128]{2,1,0:T(8,128)(2,1)S(1)} %copy-done), kind=kOutput, calls=%fused_computation.102 | convolution fusion | flops 402653184 | bytes 2621440 | tf_op jit(solution)/shard_map/hts,hsp->htp/dot_general | solution.py:158
  65.0 13.6 %while.49 = (s32[]{:T(128)}, f32[2,1024]{1,0:T(2,128)S(1)}, f32[2,1024]{1,0:T(2,128)S(1)}, f32[2,1024,128]{2,1,0:T(8,128)S(1)}, bf16[2,512,256]{2,1,0:T(8,128)(2...) while((s32[]{:T(128)}, f32[2,1024]{1,0:T(2,128)S(1)}, ...), condition=%wide.region_7.8_spmd.clone, body=%wide.region_4.7_spmd.clone.sunk | while | flops 137505920 | bytes 6563051 | solution.py:92
  65.3 1.2 fusion.86
  66.8 1.6 %convolution_add_fusion.5 = f32[2,1024,128]{2,1,0:T(8,128)S(1)} fusion(f32[2,1024,128]{2,1,0:T(8,128)S(1)} %get-tuple-element.598, f32[2,1024,128]{1,2,0:T(8,128)S(1)} %get-tuple-element.553, f32[2,1024]{1,0:T(2,128)S(1)} %get-tuple-element.555, f32[2,1024]{1,0:T(2,128)S(1)} %fusion.87, pred[]{:T(512)S(6)} %compare.10, ...), kind=kOutput, calls=%fused_computation.14.clone.1 | convolution fusion | flops 68681728 | bytes 3358729 | tf_op jit(solution)/shard_map/while/body/eval_jaxpr/grk,gkd->grd/dot_general | solution.py:84
  68.7 1.2 fusion.86
  70.2 1.6 %convolution_add_fusion.5 = f32[2,1024,128]{2,1,0:T(8,128)S(1)} fusion(f32[2,1024,128]{2,1,0:T(8,128)S(1)} %get-tuple-element.598, f32[2,1024,128]{1,2,0:T(8,128)S(1)} %get-tuple-element.553, f32[2,1024]{1,0:T(2,128)S(1)} %get-tuple-element.555, f32[2,1024]{1,0:T(2,128)S(1)} %fusion.87, pred[]{:T(512)S(6)} %compare.10, ...), kind=kOutput, calls=%fused_computation.14.clone.1 | convolution fusion | flops 68681728 | bytes 3358729 | tf_op jit(solution)/shard_map/while/body/eval_jaxpr/grk,gkd->grd/dot_general | solution.py:84
  72.1 1.2 fusion.86
  73.6 1.6 %convolution_add_fusion.5 = f32[2,1024,128]{2,1,0:T(8,128)S(1)} fusion(f32[2,1024,128]{2,1,0:T(8,128)S(1)} %get-tuple-element.598, f32[2,1024,128]{1,2,0:T(8,128)S(1)} %get-tuple-element.553, f32[2,1024]{1,0:T(2,128)S(1)} %get-tuple-element.555, f32[2,1024]{1,0:T(2,128)S(1)} %fusion.87, pred[]{:T(512)S(6)} %compare.10, ...), kind=kOutput, calls=%fused_computation.14.clone.1 | convolution fusion | flops 68681728 | bytes 3358729 | tf_op jit(solution)/shard_map/while/body/eval_jaxpr/grk,gkd->grd/dot_general | solution.py:84
  75.5 1.2 fusion.86
  77.0 1.6 %convolution_add_fusion.5 = f32[2,1024,128]{2,1,0:T(8,128)S(1)} fusion(f32[2,1024,128]{2,1,0:T(8,128)S(1)} %get-tuple-element.598, f32[2,1024,128]{1,2,0:T(8,128)S(1)} %get-tuple-element.553, f32[2,1024]{1,0:T(2,128)S(1)} %get-tuple-element.555, f32[2,1024]{1,0:T(2,128)S(1)} %fusion.87, pred[]{:T(512)S(6)} %compare.10, ...), kind=kOutput, calls=%fused_computation.14.clone.1 | convolution fusion | flops 68681728 | bytes 3358729 | tf_op jit(solution)/shard_map/while/body/eval_jaxpr/grk,gkd->grd/dot_general | solution.py:84
  78.7 0.3 divide_convert_fusion
  79.0 1.0 copy.91
  80.0 3.5 %all-to-all-start.1 = ((bf16[2,8,128,128]{2,3,0,1:T(8,128)(2,1)}), bf16[2,8,128,128]{2,3,0,1:T(8,128)(2,1)S(1)}, u32[]{:S(2)}, u32[]{:S(2)}) async-start(bf16[2,8,128,128]{2,3,0,1:T(8,128)(2,1)} %copy.91), calls=%async_computation.1 | async-start | bytes 1048576 | tf_op jit(solution)/shard_map/all_to_all | solution.py:132
  83.9 1.1 copy-done.14
  85.1 3.3 %multiply_reduce_fusion.3 = (f32[16,128]{1,0:T(8,128)S(1)}, f32[16,128,128]{1,2,0:T(8,128)S(1)}) fusion(bf16[16,128,128]{1,2,0:T(8,128)(2,1)S(1)} %copy.88, f32[16]{0:T(128)S(1)} %copy-done.18, f32[16,128,128]{1,2,0:T(8,128)} %fusion.49, f32[16,128,64]{1,2,0:T(8,128)S(1)} %bitcast.93, f32[16,64,128]{2,1,0:T(8,128)S(1)} %get-tuple-element.293, ...), kind=kOutput, calls=%fused_computation.67 | convolution fusion | flops 203421696 | bytes 4210816 | tf_op jit(solution)/shard_map/htn,hnp->htp/dot_general | solution.py:168
  88.4 5.4 %all-to-all-done.1 = bf16[2,8,128,128]{2,3,0,1:T(8,128)(2,1)S(1)} async-done(((bf16[2,8,128,128]{2,3,0,1:T(8,128)(2,1)}), bf16[2,8,128,128]{2,3,0,1:T(8,128)(2,1)S(1)}, u32[]{:S(2)}, u32[]{:S(2)}) %all-to-all-start.1) | async-done | bytes 524320 | tf_op jit(solution)/shard_map/all_to_all | solution.py:132
  94.0 0.4 multiply_reduce_fusion.1
  94.4 0.6 multiply_reduce_fusion
  95.0 0.5 copy-done.7
  95.5 2.8 %convolution_convert_fusion = bf16[16,64,128]{2,1,0:T(8,128)(2,1)} fusion(f32[16,128,128]{1,2,0:T(8,128)S(1)} %get-tuple-element.394, f32[16,128,64]{1,2,0:T(8,128)S(1)} %bitcast.94, f32[16,128]{1,0:T(8,128)S(1)} %get-tuple-element.404), kind=kOutput, calls=%fused_computation.51 | convolution fusion | flops 201588736 | bytes 1843200 | tf_op jit(solution)/shard_map/htn,htp->hnp/dot_general | solution.py:185
  98.3 2.2 %fusion.28 = (f32[16,128]{1,0:T(8,128)S(1)}, f32[16,128,128]{1,2,0:T(8,128)}) fusion(bf16[16,128,128]{1,2,0:T(8,128)(2,1)S(1)} %copy.88, f32[16,128,128]{2,1,0:T(8,128)S(1)} %copy-done.3, f32[16,128,128]{1,2,0:T(8,128)S(1)} %get-tuple-element.394), kind=kOutput, calls=%fused_computation.54 | convolution fusion | flops 403437568 | bytes 3678208 | tf_op jit(solution)/shard_map/hts,htp->hsp/dot_general | solution.py:176
  100.9 10.3 %all-reduce.1 = bf16[64]{0:T(256)(128)(2,1)S(1)} all-reduce(bf16[64]{0:T(256)(128)(2,1)S(1)} %dynamic-update-slice.1), channel_id=5, replica_groups=mesh['groups'=2,'seq'=4,'head'=2,'sub'=2] {'seq'}, use_global_device_ids=true, to_apply=%add.1 | all-reduce | flops 64 | bytes 256
  111.2 2.2 %convolution_multiply_fusion.3 = f32[16,128,64]{1,2,0:T(8,128)S(1)} fusion(f32[16,128,128]{1,2,0:T(8,128)S(1)} %get-tuple-element.394, f32[16,128]{1,0:T(8,128)S(1)} %get-tuple-element.404, f32[16,64,128]{2,1,0:T(8,128)S(1)} %get-tuple-element.293, f32[16,64,128]{2,1,0:T(8,128)} %param.19, f32[16]{0:T(128)S(1)} %get-tuple-element.294), kind=kOutput, calls=%fused_computation.46 | convolution fusion | flops 201719808 | bytes 2629696 | tf_op jit(solution)/shard_map/hnp,htp->htn/dot_general | solution.py:181
  113.4 1.2 convolution_multiply_fusion.1
  114.7 1.0 copy-done.4
  115.7 2.9 %convolution_add_fusion.2 = f32[16,128,64]{1,2,0:T(8,128)} fusion(f32[16,128,64]{1,2,0:T(8,128)S(1)} %convolution_multiply_fusion.3, f32[16,128,128]{2,1,0:T(8,128)S(1)} %convolution_multiply_fusion.1, f32[16,128,64]{1,2,0:T(8,128)S(1)} %bitcast.97), kind=kOutput, calls=%fused_computation.47 | convolution fusion | flops 201457664 | bytes 2621440 | tf_op jit(solution)/shard_map/hts,hsn->htn/dot_general | solution.py:180
  118.6 7.5 %all-gather.9.cloned.1.call-done = bf16[64,64,128]{2,1,0:T(8,128)(2,1)} async-done(((bf16[16,64,128]{2,1,0:T(8,128)(2,1)}), bf16[64,64,128]{2,1,0:T(8,128)(2,1)}) %all-gather.9.cloned.1.call-update) | async-done | bytes 1048592 | tf_op jit(solution)/shard_map/all_gather | solution.py:36
  126.1 4.4 %while.48 = (s32[]{:T(128)}, f32[16,64,128]{2,1,0:T(8,128)S(1)}, f32[16]{0:T(128)S(1)}, s32[]{:T(128)}, bf16[4,16]{1,0:T(4,128)(2,1)S(1)}, /*index=5*/bf16[4,16,...) while((s32[]{:T(128)}, f32[16,64,128]{2,1,0:T(8,128)S(1)}, ...), condition=%wide.region_15.16_spmd, body=%wide.region_13.15_spmd.sunk | while | flops 786486 | bytes 1573487 | solution.py:53
  126.2 1.3 fusion.81
  127.5 1.3 fusion.81
  128.9 1.3 fusion.81
  130.5 1.1 fusion.26
  131.7 2.8 %fusion.29 = (f32[16,128]{1,0:T(8,128)S(1)}, bf16[16,128,128]{1,2,0:T(8,128)(2,1)}) fusion(bf16[16,128,128]{1,2,0:T(8,128)(2,1)S(1)} %copy.88, f32[16,128,128]{1,2,0:T(8,128)S(1)} %get-tuple-element.394, f32[16]{0:T(128)S(1)} %copy-done.18, f32[16,128,128]{1,2,0:T(8,128)S(1)} %copy-done.11, f32[16,64,128]{2,1,0:T(8,128)S(1)} %get-tuple-element.297, ...), kind=kOutput, calls=%fused_computation.55 | convolution fusion | flops 203290624 | bytes 4210752 | tf_op jit(solution)/shard_map/hsn,hnp->hsp/dot_general | solution.py:198
  134.5 1.0 convolution_add_fusion.3
  135.7 0.7 copy.98
  136.6 1.0 copy.97
  137.6 1.2 reduce_window_sum.22
  138.9 0.7 broadcast_add_fusion
  (111 shorter events, 5.6 us)
Async XLA Ops:
  7.2 1.4 copy-start.15
  7.2 1.7 %copy-start = (bf16[16,128,128]{2,1,0:T(8,128)(2,1)S(1)}, bf16[16,128,128]{2,1,0:T(8,128)(2,1)}, u32[]{:S(2)}) copy-start(bf16[16,128,128]{2,1,0:T(8,128)(2,1)} %param.15) | copy-start | bytes 1572868
  7.2 76.4 %all-gather.7.cloned.1.call-start = ((), (), s32[]{:S(2)}) async-start(), calls=%async_computation.2 | async-start | bytes 1310720 | tf_op jit(solution)/shard_map/all_gather | solution.py:14
  8.8 1.3 copy-start.9
  8.8 1.3 copy-start.16
  10.9 54.0 %all-to-all-start = ((bf16[2,8,128,128]{3,2,0,1:T(8,128)(2,1)}), bf16[2,8,128,128]{3,2,0,1:T(8,128)(2,1)S(1)}, u32[]{:S(2)}, u32[]{:S(2)}) async-start(bf16[2,8,128,128]{3,2,0,1:T(8,128)(2,1)} %copy.89), calls=%async_computation | async-start | bytes 1048576 | tf_op jit(solution)/shard_map/all_to_all | solution.py:124
  17.8 0.7 copy-start.19
  38.4 0.9 copy-start.17
  38.8 24.0 %copy-start.2 = (f32[16,128,128]{2,1,0:T(8,128)}, f32[16,128,128]{2,1,0:T(8,128)S(1)}, u32[]{:S(2)}) copy-start(f32[16,128,128]{2,1,0:T(8,128)S(1)} %bitcast_multiply_fusion.1) | copy-start | bytes 3145732
  80.0 13.7 %all-to-all-start.1 = ((bf16[2,8,128,128]{2,3,0,1:T(8,128)(2,1)}), bf16[2,8,128,128]{2,3,0,1:T(8,128)(2,1)S(1)}, u32[]{:S(2)}, u32[]{:S(2)}) async-start(bf16[2,8,128,128]{2,3,0,1:T(8,128)(2,1)} %copy.91), calls=%async_computation.1 | async-start | bytes 1048576 | tf_op jit(solution)/shard_map/all_to_all | solution.py:132
  83.5 42.5 %all-gather.9.cloned.1.call-start = ((), (), s32[]{:S(2)}) async-start(), calls=%async_computation.3 | async-start | bytes 1310720 | tf_op jit(solution)/shard_map/all_gather | solution.py:36
  83.8 1.2 copy-start.14
  83.9 4.4 %copy-start.6 = (f32[2,8,128,64]{2,3,1,0:T(8,128)}, f32[2,8,128,64]{2,3,1,0:T(8,128)S(1)}, u32[]{:S(2)}) copy-start(f32[2,8,128,64]{2,3,1,0:T(8,128)S(1)} %broadcast_in_dim.109) | copy-start | bytes 1572868
  83.9 1.2 copy-start.18
  94.4 1.0 copy-start.7
  95.5 2.9 %copy-start.3 = (f32[16,128,128]{2,1,0:T(8,128)S(1)}, f32[16,128,128]{2,1,0:T(8,128)}, u32[]{:S(2)}) copy-start(f32[16,128,128]{2,1,0:T(8,128)} %copy-done.2) | copy-start | bytes 3145732
  111.2 2.2 %copy-start.1 = (bf16[16,128,128]{2,1,0:T(8,128)(2,1)S(1)}, bf16[16,128,128]{2,1,0:T(8,128)(2,1)}, u32[]{:S(2)}) copy-start(bf16[16,128,128]{2,1,0:T(8,128)(2,1)} %param.15) | copy-start | bytes 1572868
  113.4 2.2 %copy-start.10 = (f32[2,8,128,64]{2,3,1,0:T(8,128)S(1)}, f32[2,8,128,64]{2,3,1,0:T(8,128)}, u32[]{:S(2)}) copy-start(f32[2,8,128,64]{2,3,1,0:T(8,128)} %copy-done.9) | copy-start | bytes 1572868
  114.7 1.0 copy-start.4
  130.5 1.2 copy-start.11
  131.7 2.8 %copy-start.5 = (f32[16,128,128]{2,1,0:T(8,128)S(1)}, f32[16,128,128]{2,1,0:T(8,128)}, u32[]{:S(2)}) copy-start(f32[16,128,128]{2,1,0:T(8,128)} %copy-done.4) | copy-start | bytes 3145732
  131.7 2.8 %copy-start.8 = (f32[2,8,128,64]{2,3,1,0:T(8,128)S(1)}, f32[2,8,128,64]{2,3,1,0:T(8,128)}, u32[]{:S(2)}) copy-start(f32[2,8,128,64]{2,3,1,0:T(8,128)} %copy-done.6) | copy-start | bytes 1572868
  134.5 1.1 copy-start.12
  135.6 1.0 copy-start.13
Sparse Core Ops, SparseCore 0:
  10.2 41.8 all-gather.6
  98.5 27.5 all-gather.8
where the time goes:
time: 147 us; the launch traced here: 146 us
  blocking collectives  51.8 us (35%)
  matrix products  34.5 us (23%)
  between operations  15.2 us (10%)
  waiting for transfers between devices  12.9 us (9%)
  other arithmetic  11.2 us (8%)
  local copies, waits for them, and re-layouts  10.1 us (7%)
  starting transfers between devices  9.87 us (7%)
    unnamed x2, blocking collectives  28.3 us
    all_gather x1, blocking collectives, attend(): shards = lax.all_gather(keys_values, 'seq', axis=1, tiled=True)  23.4 us
    unnamed x51, local copies, waits for them, and re-layouts  7.57 us
    all_gather x1, waiting for transfers between devices, prefix(): lax.all_gather(a.astype(kind), axis)  7.49 us
    dot_general x4, matrix products, one_block(): jnp.einsum('grk,gkd->grd', weights.astype(jnp.bfloat16), key_block[:, :,...  6.51 us
    all_to_all x1, starting transfers between devices, body(): lax.all_to_all(sectioned, 'seq', split_axis=1, concat_axis=1, tiled=True)  6.32 us
    all_to_all x1, waiting for transfers between devices, body(): lax.all_to_all(answers, 'seq', split_axis=1, concat_axis=1, tiled=True)  5.39 us
    dot_general x4, matrix products, one_block(): jnp.einsum('grd,gkd->grk', query_rows, key_block[:, :, :head_width], pref...  4.86 us
  transfers between devices with their start and end apart: 4, of which 2 were waited for; matrix products, arithmetic and copies ran while one was open for 22% of the time, Pallas kernels for 0%

commit v1 on v0

--- a/solution.py
+++ b/solution.py
@@ -59,7 +59,13 @@
     start_max = jnp.full((group_count, row_count), -1e30, jnp.float32)
     start_sum = jnp.zeros((group_count, row_count), jnp.float32)
     start_acc = jnp.zeros((group_count, row_count, head_width), jnp.float32)
-    shards = lax.all_gather(keys_values, "seq", axis=1, tiled=True)
+    size = lax.axis_size("seq")
+    held, pieces = (keys_values, [keys_values])
+    for _ in range(size - 1):
+        held = lax.ppermute(held, "seq", [(i, (i + 1) % size) for i in range(size)])
+        pieces.insert(0, held)
+    row_of_blocks = jnp.concatenate(pieces, axis=1)
+    shards = jnp.roll(row_of_blocks, (lax.axis_index("seq") + 1) * keys_values.shape[1], axis=1)
     block_rows = math.gcd(shards.shape[1], tok_dev)
 
     def one_block(number, running):

time: 147 us -> 142 us (0.966)
  blocking collectives: 51.8 us -> 28.7 us
  waiting for transfers between devices: 12.9 us -> 22.9 us
  local copies, waits for them, and re-layouts: 10.1 us -> 13.6 us
  starting transfers between devices: 9.87 us -> 13.2 us
    all_gather x1 -> x0, blocking collectives: 23.4 us -> none  [attend(): shards = lax.all_gather(keys_values, 'seq', axis=1, tiled=True)]
    ppermute x0 -> x3, waiting for transfers between devices: none -> 16.3 us  [attend(): held = lax.ppermute(held, 'seq', [(i, (i + 1) % size) for i in range(size)])]
    ppermute x0 -> x3, starting transfers between devices: none -> 5.66 us  [attend(): held = lax.ppermute(held, 'seq', [(i, (i + 1) % size) for i in range(size)])]
    all_to_all x1, waiting for transfers between devices: 5.39 us -> 0.01 us  [body(): lax.all_to_all(answers, 'seq', split_axis=1, concat_axis=1, tiled=True)]
    all_to_all x1, starting transfers between devices: 6.32 us -> 3.99 us  [body(): lax.all_to_all(sectioned, 'seq', split_axis=1, concat_axis=1, tiled=True)]
    unnamed x51 -> x50, local copies, waits for them, and re-layouts: 7.57 us -> 9.14 us
  transfers between devices with their start and end apart: 4 -> 7, of which waited for: 2 -> 3; matrix products, arithmetic and copies ran while one was open for 22% -> 24% of each run, Pallas kernels for 0% -> 0%
where the time goes in v1:
time: 142 us; the launch traced here: 140 us
  matrix products  35.8 us (25%)
  blocking collectives  28.7 us (20%)
  waiting for transfers between devices  22.9 us (16%)
  between operations  15.1 us (11%)
  local copies, waits for them, and re-layouts  13.6 us (10%)
  starting transfers between devices  13.2 us (9%)
  other arithmetic  10.5 us (7%)
    unnamed x2, blocking collectives  28.7 us
    ppermute x3, waiting for transfers between devices, attend(): held = lax.ppermute(held, 'seq', [(i, (i + 1) % size) for i in range(size)])  16.3 us
    unnamed x50, local copies, waits for them, and re-layouts  9.14 us
    dot_general x4, matrix products, one_block(): jnp.einsum('grk,gkd->grd', weights.astype(jnp.bfloat16), key_block[:, :,...  6.52 us
    all_gather x1, waiting for transfers between devices, prefix(): lax.all_gather(a.astype(kind), axis)  6.48 us
    ppermute x3, starting transfers between devices, attend(): held = lax.ppermute(held, 'seq', [(i, (i + 1) % size) for i in range(size)])  5.66 us
    dot_general x4, matrix products, one_block(): jnp.einsum('grd,gkd->grk', query_rows, key_block[:, :, :head_width], pref...  4.86 us
    all_to_all x1, starting transfers between devices, body(): lax.all_to_all(sectioned, 'seq', split_axis=1, concat_axis=1, tiled=True)  3.99 us
  transfers between devices with their start and end apart: 7, of which 3 were waited for; matrix products, arithmetic and copies ran while one was open for 24% of the time, Pallas kernels for 0%

profile of v1, /device:TPU:0, one launch (start us, length us, event | category | flops | bytes accessed | tf_op | source)
XLA Modules:
  0.0 140.5 jit_solution(10552049607273684000)
XLA Ops:
  7.2 3.1 %collective-permute-start = (bf16[2,128,256]{2,1,0:T(8,128)(2,1)}, bf16[2,128,256]{2,1,0:T(8,128)(2,1)S(1)}, u32[]{:S(2)}, u32[]{:S(2)}) collective-permute-start(bf16[2,128,256]{2,1,0:T(8,128)(2,1)} %param.14), channel_id=1, source_target_pairs={{0,4},{4,8},{8,12},{12,0},{1,5},{5,9},{9,13},{13,1},{2,6},{6,10},{... | collective-permute-start | bytes 393224 | tf_op jit(solution)/shard_map/ppermute | solution.py:65
  10.2 1.9 %copy.89 = bf16[2,8,128,128]{3,2,0,1:T(8,128)(2,1)} copy(bf16[2,8,128,128]{3,2,1,0:T(8,128)(2,1)} %bitcast.102) | data formatting | bytes 1048576 | tf_op jit(solution)/shard_map/reshape | solution.py:129
  12.2 4.0 %all-to-all-start = ((bf16[2,8,128,128]{3,2,0,1:T(8,128)(2,1)}), bf16[2,8,128,128]{3,2,0,1:T(8,128)(2,1)S(1)}, u32[]{:S(2)}, u32[]{:S(2)}) async-start(bf16[2,8,128,128]{3,2,0,1:T(8,128)(2,1)} %copy.89), calls=%async_computation | async-start | bytes 1048576 | tf_op jit(solution)/shard_map/all_to_all | solution.py:130
  16.9 2.1 %collective-permute-start.1 = (bf16[2,128,256]{2,1,0:T(8,128)(2,1)S(1)}, bf16[2,128,256]{2,1,0:T(8,128)(2,1)S(1)}, u32[]{:S(2)}, u32[]{:S(2)}) collective-permute-start(bf16[2,128,256]{2,1,0:T(8,128)(2,1)S(1)} %collective-permute-done), channel_id=1, source_target_pairs={{0,4},{4,8},{8,12},{12,0},{1,5},{5,9},{9,13},{13,1},{2,6},{6,10},{... | collective-permute-start | bytes 393224 | tf_op jit(solution)/shard_map/ppermute | solution.py:65
  19.0 12.3 %collective-permute-done.1 = bf16[2,128,256]{2,1,0:T(8,128)(2,1)S(1)} collective-permute-done((bf16[2,128,256]{2,1,0:T(8,128)(2,1)S(1)}, bf16[2,128,256]{2,1,0:T(8,128)(2,1)S(1)}, u32[]{:S(2)}, u32[]{:S(2)}) %collective-permute-start.1) | collective-permute-done | bytes 131104 | tf_op jit(solution)/shard_map/ppermute | solution.py:65
  31.9 0.8 copy-done.4
  32.7 1.3 convolution_convert_fusion.1
  34.0 4.0 %collective-permute-done.2 = bf16[2,128,256]{2,1,0:T(8,128)(2,1)S(1)} collective-permute-done((bf16[2,128,256]{2,1,0:T(8,128)(2,1)S(1)}, bf16[2,128,256]{2,1,0:T(8,128)(2,1)S(1)}, u32[]{:S(2)}, u32[]{:S(2)}) %collective-permute-start.2) | collective-permute-done | bytes 131104 | tf_op jit(solution)/shard_map/ppermute | solution.py:65
  38.1 0.9 copy-done.12
  39.1 0.8 constant_dynamic-slice_fusion.2
  40.0 13.6 %while.49 = (s32[]{:T(128)}, f32[2,1024]{1,0:T(2,128)S(1)}, f32[2,1024]{1,0:T(2,128)S(1)}, f32[2,1024,128]{2,1,0:T(8,128)S(1)}, bf16[2,512,256]{2,1,0:T(8,128)(2...) while((s32[]{:T(128)}, f32[2,1024]{1,0:T(2,128)S(1)}, ...), condition=%wide.region_7.8_spmd.clone, body=%wide.region_4.7_spmd.clone.sunk | while | flops 137505920 | bytes 6563051 | solution.py:98
  40.2 1.2 fusion.86
  41.7 1.6 %convolution_add_fusion.5 = f32[2,1024,128]{2,1,0:T(8,128)S(1)} fusion(f32[2,1024,128]{2,1,0:T(8,128)S(1)} %get-tuple-element.598, f32[2,1024,128]{1,2,0:T(8,128)S(1)} %get-tuple-element.553, f32[2,1024]{1,0:T(2,128)S(1)} %get-tuple-element.555, f32[2,1024]{1,0:T(2,128)S(1)} %fusion.87, pred[]{:T(512)S(6)} %compare.11, ...), kind=kOutput, calls=%fused_computation.14.clone.1 | convolution fusion | flops 68681728 | bytes 3358729 | tf_op jit(solution)/shard_map/while/body/eval_jaxpr/grk,gkd->grd/dot_general | solution.py:90
  43.6 1.2 fusion.86
  45.1 1.6 %convolution_add_fusion.5 = f32[2,1024,128]{2,1,0:T(8,128)S(1)} fusion(f32[2,1024,128]{2,1,0:T(8,128)S(1)} %get-tuple-element.598, f32[2,1024,128]{1,2,0:T(8,128)S(1)} %get-tuple-element.553, f32[2,1024]{1,0:T(2,128)S(1)} %get-tuple-element.555, f32[2,1024]{1,0:T(2,128)S(1)} %fusion.87, pred[]{:T(512)S(6)} %compare.11, ...), kind=kOutput, calls=%fused_computation.14.clone.1 | convolution fusion | flops 68681728 | bytes 3358729 | tf_op jit(solution)/shard_map/while/body/eval_jaxpr/grk,gkd->grd/dot_general | solution.py:90
  47.0 1.2 fusion.86
  48.6 1.6 %convolution_add_fusion.5 = f32[2,1024,128]{2,1,0:T(8,128)S(1)} fusion(f32[2,1024,128]{2,1,0:T(8,128)S(1)} %get-tuple-element.598, f32[2,1024,128]{1,2,0:T(8,128)S(1)} %get-tuple-element.553, f32[2,1024]{1,0:T(2,128)S(1)} %get-tuple-element.555, f32[2,1024]{1,0:T(2,128)S(1)} %fusion.87, pred[]{:T(512)S(6)} %compare.11, ...), kind=kOutput, calls=%fused_computation.14.clone.1 | convolution fusion | flops 68681728 | bytes 3358729 | tf_op jit(solution)/shard_map/while/body/eval_jaxpr/grk,gkd->grd/dot_general | solution.py:90
  50.5 1.2 fusion.86
  52.0 1.6 %convolution_add_fusion.5 = f32[2,1024,128]{2,1,0:T(8,128)S(1)} fusion(f32[2,1024,128]{2,1,0:T(8,128)S(1)} %get-tuple-element.598, f32[2,1024,128]{1,2,0:T(8,128)S(1)} %get-tuple-element.553, f32[2,1024]{1,0:T(2,128)S(1)} %get-tuple-element.555, f32[2,1024]{1,0:T(2,128)S(1)} %fusion.87, pred[]{:T(512)S(6)} %compare.11, ...), kind=kOutput, calls=%fused_computation.14.clone.1 | convolution fusion | flops 68681728 | bytes 3358729 | tf_op jit(solution)/shard_map/while/body/eval_jaxpr/grk,gkd->grd/dot_general | solution.py:90
  54.0 1.0 copy.91
  55.0 3.5 %all-to-all-start.1 = ((bf16[2,8,128,128]{2,3,0,1:T(8,128)(2,1)}), bf16[2,8,128,128]{2,3,0,1:T(8,128)(2,1)S(1)}, u32[]{:S(2)}, u32[]{:S(2)}) async-start(bf16[2,8,128,128]{2,3,0,1:T(8,128)(2,1)} %copy.91), calls=%async_computation.1 | async-start | bytes 1048576 | tf_op jit(solution)/shard_map/all_to_all | solution.py:138
  58.8 0.6 copy-done.15
  59.5 0.6 dynamic-slice
  61.0 13.5 %all-reduce = bf16[64]{0:T(256)(128)(2,1)S(1)} all-reduce(bf16[64]{0:T(256)(128)(2,1)S(1)} %dynamic-update-slice), channel_id=2, replica_groups=mesh['groups'=2,'seq'=4,'head'=2,'sub'=2] {'seq'}, use_global_device_ids=true, to_apply=%add | all-reduce | flops 64 | bytes 256
  75.3 1.0 copy-done.1
  76.3 2.3 %fusion.49 = f32[16,128,128]{1,2,0:T(8,128)} fusion(f32[16,128,128]{2,1,0:T(8,128)S(1)} %bitcast_multiply_fusion.1, bf16[16,128,128]{2,1,0:T(8,128)(2,1)S(1)} %copy-done), kind=kOutput, calls=%fused_computation.111 | convolution fusion | flops 402653184 | bytes 2621440 | tf_op jit(solution)/shard_map/hts,hsp->htp/dot_general | solution.py:164
  79.1 1.0 copy-done.10
  80.0 3.3 %multiply_reduce_fusion.3 = (f32[16,128]{1,0:T(8,128)S(1)}, f32[16,128,128]{1,2,0:T(8,128)S(1)}) fusion(bf16[16,128,128]{1,2,0:T(8,128)(2,1)S(1)} %copy.88, f32[16]{0:T(128)S(1)} %copy-done.14, f32[16,128,128]{1,2,0:T(8,128)} %fusion.49, f32[16,128,64]{1,2,0:T(8,128)S(1)} %bitcast.93, f32[16,64,128]{2,1,0:T(8,128)S(1)} %get-tuple-element.293, ...), kind=kOutput, calls=%fused_computation.67 | convolution fusion | flops 203421696 | bytes 4210816 | tf_op jit(solution)/shard_map/htn,hnp->htp/dot_general | solution.py:174
  83.9 0.6 multiply_reduce_fusion
  84.5 2.8 %convolution_convert_fusion = bf16[16,64,128]{2,1,0:T(8,128)(2,1)} fusion(f32[16,128,128]{1,2,0:T(8,128)S(1)} %get-tuple-element.394, f32[16,128,64]{1,2,0:T(8,128)S(1)} %bitcast.94, f32[16,128]{1,0:T(8,128)S(1)} %get-tuple-element.404), kind=kOutput, calls=%fused_computation.51 | convolution fusion | flops 201588736 | bytes 1843200 | tf_op jit(solution)/shard_map/htn,htp->hnp/dot_general | solution.py:191
  87.3 3.3 %fusion.28 = (f32[16,128]{1,0:T(8,128)S(1)}, f32[16,128,128]{1,2,0:T(8,128)}) fusion(bf16[16,128,128]{1,2,0:T(8,128)(2,1)S(1)} %copy.88, f32[16,128,128]{2,1,0:T(8,128)} %copy-done.1, f32[16,128,128]{1,2,0:T(8,128)S(1)} %get-tuple-element.394), kind=kOutput, calls=%fused_computation.54 | convolution fusion | flops 403437568 | bytes 3678208 | tf_op jit(solution)/shard_map/hts,htp->hsp/dot_general | solution.py:182
  91.0 15.1 %all-reduce.1 = bf16[64]{0:T(256)(128)(2,1)S(1)} all-reduce(bf16[64]{0:T(256)(128)(2,1)S(1)} %dynamic-update-slice.1), channel_id=5, replica_groups=mesh['groups'=2,'seq'=4,'head'=2,'sub'=2] {'seq'}, use_global_device_ids=true, to_apply=%add.1 | all-reduce | flops 64 | bytes 256
  106.3 2.1 %convolution_multiply_fusion.3 = f32[16,128,64]{1,2,0:T(8,128)S(1)} fusion(f32[16,128,128]{1,2,0:T(8,128)S(1)} %get-tuple-element.394, f32[16,128]{1,0:T(8,128)S(1)} %get-tuple-element.404, f32[16,64,128]{2,1,0:T(8,128)S(1)} %get-tuple-element.293, f32[16,64,128]{2,1,0:T(8,128)} %param.19, f32[16]{0:T(128)S(1)} %get-tuple-element.294), kind=kOutput, calls=%fused_computation.46 | convolution fusion | flops 201719808 | bytes 2629696 | tf_op jit(solution)/shard_map/hnp,htp->htn/dot_general | solution.py:187
  108.4 1.2 convolution_multiply_fusion.1
  109.6 1.0 copy-done.2
  110.6 2.9 %convolution_add_fusion.2 = f32[16,128,64]{1,2,0:T(8,128)} fusion(f32[16,128,64]{1,2,0:T(8,128)S(1)} %convolution_multiply_fusion.3, f32[16,128,128]{2,1,0:T(8,128)S(1)} %convolution_multiply_fusion.1, f32[16,128,64]{1,2,0:T(8,128)S(1)} %bitcast.97), kind=kOutput, calls=%fused_computation.47 | convolution fusion | flops 201457664 | bytes 2621440 | tf_op jit(solution)/shard_map/hts,hsn->htn/dot_general | solution.py:186
  113.5 6.5 %all-gather.9.cloned.1.call-done = bf16[64,64,128]{2,1,0:T(8,128)(2,1)} async-done(((bf16[16,64,128]{2,1,0:T(8,128)(2,1)}), bf16[64,64,128]{2,1,0:T(8,128)(2,1)}) %all-gather.9.cloned.1.call-update) | async-done | bytes 1048592 | tf_op jit(solution)/shard_map/all_gather | solution.py:36
  120.1 4.4 %while.48 = (s32[]{:T(128)}, f32[16,64,128]{2,1,0:T(8,128)S(1)}, f32[16]{0:T(128)S(1)}, s32[]{:T(128)}, bf16[4,16]{1,0:T(4,128)(2,1)S(1)}, /*index=5*/bf16[4,16,...) while((s32[]{:T(128)}, f32[16,64,128]{2,1,0:T(8,128)S(1)}, ...), condition=%wide.region_15.16_spmd, body=%wide.region_13.15_spmd.sunk | while | flops 786486 | bytes 1573487 | solution.py:53
  120.1 1.3 fusion.81
  121.5 1.3 fusion.81
  122.9 1.3 fusion.81
  124.5 1.1 fusion.26
  125.8 2.8 %fusion.29 = (f32[16,128]{1,0:T(8,128)S(1)}, bf16[16,128,128]{1,2,0:T(8,128)(2,1)}) fusion(bf16[16,128,128]{1,2,0:T(8,128)(2,1)S(1)} %copy.88, f32[16,128,128]{1,2,0:T(8,128)S(1)} %get-tuple-element.394, f32[16]{0:T(128)S(1)} %copy-done.14, f32[16,128,128]{1,2,0:T(8,128)S(1)} %copy-done.7, f32[16,64,128]{2,1,0:T(8,128)S(1)} %get-tuple-element.297, ...), kind=kOutput, calls=%fused_computation.55 | convolution fusion | flops 203290624 | bytes 4210752 | tf_op jit(solution)/shard_map/hsn,hnp->hsp/dot_general | solution.py:204
  128.6 1.0 convolution_add_fusion.3
  129.7 0.7 copy.98
  130.7 1.0 copy.97
  131.7 1.2 reduce_window_sum.22
  133.0 0.7 broadcast_add_fusion
  (117 shorter events, 7.4 us)
Async XLA Ops:
  7.2 9.7 %collective-permute-start = (bf16[2,128,256]{2,1,0:T(8,128)(2,1)}, bf16[2,128,256]{2,1,0:T(8,128)(2,1)S(1)}, u32[]{:S(2)}, u32[]{:S(2)}) collective-permute-start(bf16[2,128,256]{2,1,0:T(8,128)(2,1)} %param.14), channel_id=1, source_target_pairs={{0,4},{4,8},{8,12},{12,0},{1,5},{5,9},{9,13},{13,1},{2,6},{6,10},{... | collective-permute-start | bytes 393224 | tf_op jit(solution)/shard_map/ppermute | solution.py:65
  12.1 4.0 %copy-start.11 = (bf16[2,128,128]{2,1,0:T(8,128)(2,1)S(1)}, bf16[2,128,128]{2,1,0:T(8,128)(2,1)}, u32[]{:S(2)}) copy-start(bf16[2,128,128]{2,1,0:T(8,128)(2,1)} %param.16) | copy-start | bytes 196612
  12.2 4.1 %copy-start.13 = (f32[16,128]{1,0:T(8,128)S(1)}, f32[16,128]{1,0:T(8,128)}, u32[]{:S(2)}) copy-start(f32[16,128]{1,0:T(8,128)} %param.17) | copy-start | bytes 24580
  12.2 27.8 %all-to-all-start = ((bf16[2,8,128,128]{3,2,0,1:T(8,128)(2,1)}), bf16[2,8,128,128]{3,2,0,1:T(8,128)(2,1)S(1)}, u32[]{:S(2)}, u32[]{:S(2)}) async-start(bf16[2,8,128,128]{3,2,0,1:T(8,128)(2,1)} %copy.89), calls=%async_computation | async-start | bytes 1048576 | tf_op jit(solution)/shard_map/all_to_all | solution.py:130
  16.1 16.5 %copy-start = (bf16[16,128,128]{2,1,0:T(8,128)(2,1)S(1)}, bf16[16,128,128]{2,1,0:T(8,128)(2,1)}, u32[]{:S(2)}) copy-start(bf16[16,128,128]{2,1,0:T(8,128)(2,1)} %param.15) | copy-start | bytes 1572868
  16.1 62.6 %all-gather.7.cloned.1.call-start = ((), (), s32[]{:S(2)}) async-start(), calls=%async_computation.2 | async-start | bytes 1310720 | tf_op jit(solution)/shard_map/all_gather | solution.py:14
  16.9 14.4 %collective-permute-start.1 = (bf16[2,128,256]{2,1,0:T(8,128)(2,1)S(1)}, bf16[2,128,256]{2,1,0:T(8,128)(2,1)S(1)}, u32[]{:S(2)}, u32[]{:S(2)}) collective-permute-start(bf16[2,128,256]{2,1,0:T(8,128)(2,1)S(1)} %collective-permute-done), channel_id=1, source_target_pairs={{0,4},{4,8},{8,12},{12,0},{1,5},{5,9},{9,13},{13,1},{2,6},{6,10},{... | collective-permute-start | bytes 393224 | tf_op jit(solution)/shard_map/ppermute | solution.py:65
  31.3 6.8 %collective-permute-start.2 = (bf16[2,128,256]{2,1,0:T(8,128)(2,1)S(1)}, bf16[2,128,256]{2,1,0:T(8,128)(2,1)S(1)}, u32[]{:S(2)}, u32[]{:S(2)}) collective-permute-start(bf16[2,128,256]{2,1,0:T(8,128)(2,1)S(1)} %collective-permute-done.1), channel_id=1, source_target_pairs={{0,4},{4,8},{8,12},{12,0},{1,5},{5,9},{9,13},{13,1},{2,6},{6,10},{... | collective-permute-start | bytes 393224 | tf_op jit(solution)/shard_map/ppermute | solution.py:65
  31.9 0.8 copy-start.4
  38.1 0.9 copy-start.12
  55.0 23.6 %all-to-all-start.1 = ((bf16[2,8,128,128]{2,3,0,1:T(8,128)(2,1)}), bf16[2,8,128,128]{2,3,0,1:T(8,128)(2,1)S(1)}, u32[]{:S(2)}, u32[]{:S(2)}) async-start(bf16[2,8,128,128]{2,3,0,1:T(8,128)(2,1)} %copy.91), calls=%async_computation.1 | async-start | bytes 1048576 | tf_op jit(solution)/shard_map/all_to_all | solution.py:138
  58.5 61.6 %all-gather.9.cloned.1.call-start = ((), (), s32[]{:S(2)}) async-start(), calls=%async_computation.3 | async-start | bytes 1310720 | tf_op jit(solution)/shard_map/all_gather | solution.py:36
  58.8 0.7 copy-start.15
  75.3 1.0 copy-start.1
  79.0 1.0 copy-start.10
  79.1 1.0 copy-start.14
  108.4 2.2 %copy-start.5 = (f32[2,8,128,64]{2,3,1,0:T(8,128)S(1)}, f32[2,8,128,64]{2,3,1,0:T(8,128)}, u32[]{:S(2)}) copy-start(f32[2,8,128,64]{2,3,1,0:T(8,128)} %copy-done.4) | copy-start | bytes 1572868
  109.6 1.0 copy-start.2
  124.5 1.2 copy-start.7
  124.5 1.3 copy-start.6
  125.8 2.8 %copy-start.3 = (f32[16,128,128]{2,1,0:T(8,128)S(1)}, f32[16,128,128]{2,1,0:T(8,128)}, u32[]{:S(2)}) copy-start(f32[16,128,128]{2,1,0:T(8,128)} %copy-done.2) | copy-start | bytes 3145732
  128.6 1.0 copy-start.8
  129.7 1.0 copy-start.9
Sparse Core Ops, SparseCore 0:
  34.1 33.4 all-gather.6
  87.4 32.5 all-gather.8
